TPU v7x, 512 devices: a whole 4x4x16 slice. The times are simulated.
512 devices in a mesh: tok: 16 (over z), head: 32 (over y, x, core).
Axes of the slice: x: 4, y: 4, z: 16, core: 2. Of those that a mesh axis runs over, the one named last changes fastest.
Arguments:
- tokens: bfloat16 [3072, 4096], P(('tok', 'head')), may hold values from -6 to 6
- ln1_gain: float32 [4096], replicated, may hold values from 0.25 to 1.75
- ln1_bias: float32 [4096], replicated, may hold values from -1.75 to 1.75
- ln2_gain: float32 [4096], replicated, may hold values from 0.25 to 1.75
- ln2_bias: float32 [4096], replicated, may hold values from -1.75 to 1.75
- w_qkv: bfloat16 [4096, 12288], P('tok', 'head'), may hold values from -0.09375 to 0.09375
- b_qkv: float32 [12288], P('head'), may hold values from -3 to 3
- w_dense: bfloat16 [4096, 4096], P('head', 'tok'), may hold values from -0.09375 to 0.09375
- b_dense: float32 [4096], replicated, may hold values from -1.75 to 1.75
- w_up: bfloat16 [4096, 16384], P('tok', 'head'), may hold values from -0.09375 to 0.09375
- b_up: float32 [16384], P('head'), may hold values from -3 to 3
- w_down: bfloat16 [16384, 4096], P('head', 'tok'), may hold values from -0.046875 to 0.046875
- b_down: float32 [4096], replicated, may hold values from -1.75 to 1.75
- k_cache: bfloat16 [98304, 4096], P('tok', 'head'), may hold values from -610 to 610
- v_cache: bfloat16 [98304, 4096], P('tok', 'head'), may hold values from -6 to 6
- cache_lengths: int32 [16, 33], P('tok'), may hold values from 1 to 4096, 6144 in all within a row
Outputs:
- mixed: bfloat16 [3072, 4096], P(('tok', 'head'))
Inputs may be any that keep to these rules, and one draw needn't show every extreme that they name: `cache_lengths`: row g lists the cache lengths of group g's 33 requests in the order in which their caches lie in the group's 6144 cache rows; every row sums to 6144. Request 0 of a group is the one whose 160 new tokens are prefilled, the others decode one token each.
All inputs are finite; a program needn't handle non-finite values.
Results may differ from a plain program's by a relative error of at most 0.02.
Values may be sent and summed in bfloat16 or wider, within the bound.
No kernel may reach another device: no remote copies, remote signals or barrier semaphores. Data moves between devices by JAX's collectives and lax.ppermute only.
A program may use at most 64 MiB of HBM per device.

v0:
```python
import jax
import jax.numpy as jnp
from jax import lax
from jax.sharding import PartitionSpec as P

HD = 128
ROT = 32
WINDOW = 2048
SINKS = 4
epsilon = 1e-05


def layer_norm(values, gain, shift):
    values = values.astype(jnp.float32)
    center = jnp.mean(values, axis=-1, keepdims=True)
    spread = jnp.mean(jnp.square(values - center), axis=-1, keepdims=True)
    return (values - center) * lax.rsqrt(spread + epsilon) * gain + shift


def rotate(values, positions):
    half = ROT // 2
    inverse = jnp.power(jnp.float32(10000.0), -jnp.arange(half, dtype=jnp.float32) * (2.0 / ROT))
    angles = (
        positions.astype(jnp.float32).reshape(positions.shape + (1,) * (values.ndim - 1)) * inverse
    )
    cosine = jnp.cos(angles)
    sine = jnp.sin(angles)
    first = values[..., :half]
    second = values[..., half:ROT]
    rest = values[..., ROT:]
    return jnp.concatenate(
        [first * cosine - second * sine, second * cosine + first * sine, rest], axis=-1
    )


def token_layout(lengths_row, group_rows):
    requests_count = lengths_row.shape[0]
    count_pre = group_rows - (requests_count - 1)
    index = jnp.arange(group_rows, dtype=jnp.int32)
    owner = jnp.maximum(index - (count_pre - 1), 0)
    table = owner[:, None] == jnp.arange(requests_count, dtype=jnp.int32)[None, :]
    start = jnp.sum(jnp.where(table, lengths_row[None, :], 0), axis=1)
    place = start + jnp.where(owner == 0, index, 0)
    return (owner, place)


def slot_layout(lengths_row, slots):
    starts = jnp.cumsum(lengths_row) - lengths_row
    index = jnp.arange(slots, dtype=jnp.int32)
    inside = index[:, None] >= starts[None, :]
    owner = jnp.sum(inside.astype(jnp.int32), axis=1) - 1
    begin = jnp.max(jnp.where(inside, starts[None, :], 0), axis=1)
    return (owner, index - begin)


def visible(query_owner, query_place, key_owner, key_place):
    same = query_owner[:, None] == key_owner[None, :]
    before = key_place[None, :] <= query_place[:, None]
    near = (key_place[None, :] < SINKS) | (query_place[:, None] - key_place[None, :] < WINDOW)
    return same & before & near


def body(
    tokens,
    ln1_gain,
    ln1_bias,
    ln2_gain,
    ln2_bias,
    w_qkv,
    b_qkv,
    w_dense,
    b_dense,
    w_up,
    b_up,
    w_down,
    b_down,
    k_cache,
    v_cache,
    cache_lengths,
):
    scale = HD ** (-0.5)
    width_qkv = w_qkv.shape[1]
    width_up = w_up.shape[1]
    width_dense = w_dense.shape[0]
    packed = jnp.concatenate([w_qkv, w_up, w_dense.T, w_down.T], axis=1)
    gathered = lax.all_gather(packed, "tok", axis=0, tiled=False)
    parts = gathered.shape[0] * gathered.shape[1]
    qkv_full = gathered[:, :, :width_qkv].reshape(parts, width_qkv)
    up_full = gathered[:, :, width_qkv : width_qkv + width_up].reshape(parts, width_up)
    offset = width_qkv + width_up
    dense_t = gathered[:, :, offset : offset + width_dense].reshape(parts, width_dense)
    down_t = gathered[:, :, offset + width_dense :].reshape(parts, -1)
    whole = lax.all_gather(tokens, "head", axis=0, tiled=True)
    normed_one = layer_norm(whole, ln1_gain, ln1_bias).astype(jnp.bfloat16)
    normed_two = layer_norm(whole, ln2_gain, ln2_bias).astype(jnp.bfloat16)
    rows_total = whole.shape[0]
    projected = jnp.dot(normed_one, qkv_full, preferred_element_type=jnp.float32) + b_qkv
    upward = jnp.dot(normed_two, up_full, preferred_element_type=jnp.float32)
    lengths_row = cache_lengths[0]
    query_owner, query_place = token_layout(lengths_row, rows_total)
    queries = rotate(projected[:, :HD], query_place).astype(jnp.bfloat16)
    new_keys = rotate(projected[:, HD : 2 * HD], query_place).astype(jnp.bfloat16)
    new_values = projected[:, 2 * HD :].astype(jnp.bfloat16)
    hidden = jax.nn.gelu(upward + b_up, approximate=False).astype(jnp.bfloat16)
    slots = k_cache.shape[0]
    slot_owner, slot_place = slot_layout(lengths_row, slots)
    cache_scores = jnp.dot(queries, k_cache.T, preferred_element_type=jnp.float32) * scale
    cache_scores = jnp.where(
        visible(query_owner, query_place, slot_owner, slot_place), cache_scores, -jnp.inf
    )
    new_scores = jnp.dot(queries, new_keys.T, preferred_element_type=jnp.float32) * scale
    new_scores = jnp.where(
        visible(query_owner, query_place, query_owner, query_place), new_scores, -jnp.inf
    )
    top = jnp.maximum(jnp.max(cache_scores, axis=1), jnp.max(new_scores, axis=1))
    cache_weights = jnp.exp(cache_scores - top[:, None])
    new_weights = jnp.exp(new_scores - top[:, None])
    total = jnp.sum(cache_weights, axis=1) + jnp.sum(new_weights, axis=1)
    summed = jnp.dot(
        cache_weights.astype(jnp.bfloat16), v_cache, preferred_element_type=jnp.float32
    ) + jnp.dot(new_weights.astype(jnp.bfloat16), new_values, preferred_element_type=jnp.float32)
    attention = (summed / total[:, None]).astype(jnp.bfloat16)
    contract = (((1,), (1,)), ((), ()))
    partial = lax.dot_general(
        attention, dense_t, contract, preferred_element_type=jnp.float32
    ) + lax.dot_general(hidden, down_t, contract, preferred_element_type=jnp.float32)
    heads = lax.axis_size("head")
    partial = partial.astype(jnp.bfloat16).reshape(heads, rows_total // heads, -1)
    partial_value = lax.psum_scatter(partial, "head", scatter_dimension=0, tiled=True)
    partial_value = partial_value.reshape(tokens.shape).astype(jnp.float32)
    mixed = tokens.astype(jnp.float32) + partial_value + b_dense + b_down
    return mixed.astype(jnp.bfloat16)


def solution(mesh):
    placed = (
        P(("tok", "head"), None),
        P(),
        P(),
        P(),
        P(),
        P("tok", "head"),
        P("head"),
        P("head", "tok"),
        P(),
        P("tok", "head"),
        P("head"),
        P("head", "tok"),
        P(),
        P("tok", "head"),
        P("tok", "head"),
        P("tok", None),
    )
    return jax.shard_map(
        body, mesh=mesh, in_specs=placed, out_specs=P(("tok", "head"), None), check_vma=False
    )
```

profile of v0, /device:TPU:2, one launch (start us, length us, event | category | flops | bytes accessed | tf_op | source)
XLA Modules:
  0.0 393.0 jit_solution(7284414699249301596)
XLA Ops:
  6.5 0.7 all-gather.7.cloned.1.call-update
  7.3 1.1 copy.26
  8.4 1.1 copy.25
  9.5 1.9 pad_maximum_fusion
  11.4 0.2 reduce-window_clone.1
  11.8 0.4 convert_reduce_fusion.1
  12.2 61.5 %all-gather.7.cloned.1.call-done = bf16[32,6,4096]{2,1,0:T(8,128)(2,1)} async-done(((bf16[1,6,4096]{2,1,0:T(8,128)(2,1)}), bf16[32,6,4096]{2,1,0:T(8,128)(2,1)}) %all-gather.7.cloned.1.call-update) | async-done | bytes 1572880 | tf_op jit(solution)/shard_map/all_gather | solution.py:93
  73.7 2.1 convert_reduce_fusion
  75.8 0.1 reshape.130
  75.9 3.8 reshape.127
  79.7 2.3 multiply_reduce_fusion
  82.1 163.7 %all-gather.5.cloned.1.call-done = bf16[4096,1536]{0,1:T(8,128)(2,1)} async-done(((bf16[256,1536]{0,1:T(8,128)(2,1)}), bf16[4096,1536]{0,1:T(8,128)(2,1)}) %all-gather.5.cloned.1.call-update) | async-done | bytes 12582928 | tf_op jit(solution)/shard_map/all_gather | solution.py:86
  245.7 7.9 %copy.29 = bf16[192,8,16,256]{3,2,1,0:T(8,128)(2,1)S(1)} copy(bf16[192,8,16,256]{3,1,2,0:T(8,128)(2,1)} %bitcast.40) | data formatting | bytes 25165824
  253.8 0.2 slice.55
  254.0 1.6 copy.30
  255.6 0.3 copy-done.3
  255.9 1.2 fusion.144
  257.1 0.1 fusion.101
  257.2 0.3 fusion.146
  257.5 2.7 fusion.145
  260.2 0.2 fusion.82
  260.5 0.8 fusion.142
  261.3 0.4 copy.31
  261.7 0.6 copy-done.2
  262.3 0.8 fusion.4
  263.1 4.3 %copy.33 = bf16[64,8,16,256]{3,1,2,0:T(8,128)(2,1)} copy(bf16[64,8,16,256]{3,2,1,0:T(8,128)(2,1)S(1)} %bitcast.39) | data formatting | bytes 8388608
  267.4 4.3 %copy.32 = bf16[64,8,16,256]{3,1,2,0:T(8,128)(2,1)} copy(bf16[64,8,16,256]{3,2,1,0:T(8,128)(2,1)S(1)} %bitcast.38) | data formatting | bytes 8388608
  271.7 5.4 %fusion.32 = f32[192,4096]{1,0:T(8,128)} fusion(bf16[4096,128]{0,1:T(8,128)(2,1)S(1)} %bitcast.42, f32[192,128]{1,0:T(8,128)S(1)} %fusion.82, bf16[6144,128]{1,0:T(8,128)(2,1)S(1)} %copy-done.4, f32[192,6144]{1,0:T(8,128)} %copy-done.2, f32[192]{0:T(256)S(1)} %max.37, f32[192]{0:T(256)S(1)} %add.133), kind=kOutput, calls=%fused_computation.32 | convolution fusion | flops 505749504 | bytes 10585600 | tf_op jit(solution)/shard_map/dot_general | solution.py:124
  277.1 8.7 %fusion.1 = bf16[192,4096]{1,0:T(8,128)(2,1)S(1)} fusion(f32[192,4096]{1,0:T(8,128)} %fusion.32, bf16[4096,512]{0,1:T(8,128)(2,1)} %bitcast.43, bf16[4096,512]{0,1:T(8,128)(2,1)} %bitcast.44, f32[192,4096]{1,0:T(8,128)} %reshape.127, f32[4096]{0:T(1024)S(1)} %copy-done.11, f32[4096]{0:T(1024)S(1)} %copy-done.12, f32[192]{0:T(256)S(1)} %add_rsqrt_fusion, ...), kind=kOutput, calls=%fused_computation.3 | convolution fusion | flops 1622605824 | bytes 16289280 | tf_op jit(solution)/shard_map/dot_general | solution.py:126
  285.8 1.6 reshape.122
  287.5 97.5 %reduce-scatter.2.cloned.1.call-done = bf16[1,6,4096]{2,1,0:T(8,128)(2,1)} async-done(((bf16[32,6,4096]{2,1,0:T(8,128)(2,1)}), bf16[1,6,4096]{2,1,0:T(8,128)(2,1)}) %reduce-scatter.2.cloned.1.call-update) | async-done | bytes 49168 | tf_op jit(solution)/shard_map/reduce_scatter | solution.py:129
  385.0 1.5 fusion.81
  (48 shorter events, 0.5 us)
Async XLA Ops:
  6.5 251.0 %copy-start = (bf16[6144,128]{1,0:T(8,128)(2,1)S(1)}, bf16[6144,128]{1,0:T(8,128)(2,1)}, u32[]{:S(2)}) copy-start(bf16[6144,128]{1,0:T(8,128)(2,1)} %param.29) | copy-start | bytes 4718596
  6.5 4.9 %copy-start.8 = (s32[1,33]{1,0:T(1,128)S(1)}, s32[1,33]{1,0:T(1,128)}, u32[]{:S(2)}) copy-start(s32[1,33]{1,0:T(1,128)} %param.31) | copy-start | bytes 400
  6.5 67.2 %all-gather.7.cloned.1.call-start = ((), (), s32[]{:S(2)}) async-start(), calls=%async_computation.3 | async-start | bytes 2162688 | tf_op jit(solution)/shard_map/all_gather | solution.py:93
  7.3 238.5 %all-gather.5.cloned.1.call-start = ((), (), s32[]{:S(2)}) async-start(), calls=%async_computation.2 | async-start | bytes 13369344 | tf_op jit(solution)/shard_map/all_gather | solution.py:86
  11.4 373.6 %reduce-scatter.2.cloned.1.call-start = ((), (), s32[]{:S(2)}) async-start(), calls=%async_computation.1 | async-start | bytes 2162688 | tf_op jit(solution)/shard_map/reduce_scatter | solution.py:129
  254.0 1.9 copy-start.3
  254.0 1.9 copy-start.9
  254.0 1.9 copy-start.10
  254.0 1.9 copy-start.13
  260.2 2.2 copy-start.2
  267.4 4.3 %copy-start.4 = (bf16[6144,128]{1,0:T(8,128)(2,1)S(1)}, bf16[6144,128]{1,0:T(8,128)(2,1)}, u32[]{:S(2)}) copy-start(bf16[6144,128]{1,0:T(8,128)(2,1)} %param.30) | copy-start | bytes 4718596
  271.7 5.4 %copy-start.11 = (f32[4096]{0:T(1024)S(1)}, f32[4096]{0:T(1024)}, u32[]{:S(2)}) copy-start(f32[4096]{0:T(1024)} %param.20) | copy-start | bytes 49156
  271.7 5.4 %copy-start.12 = (f32[4096]{0:T(1024)S(1)}, f32[4096]{0:T(1024)}, u32[]{:S(2)}) copy-start(f32[4096]{0:T(1024)} %param.19) | copy-start | bytes 49156
  271.7 5.4 %copy-start.14 = (f32[512]{0:T(512)S(1)}, f32[512]{0:T(512)}, u32[]{:S(2)}) copy-start(f32[512]{0:T(512)} %param.26) | copy-start | bytes 6148
  277.1 109.4 %copy-start.1 = (bf16[6144,128]{1,0:T(8,128)(2,1)S(1)}, bf16[6144,128]{1,0:T(8,128)(2,1)}, u32[]{:S(2)}) copy-start(bf16[6144,128]{1,0:T(8,128)(2,1)} %param.29) | copy-start | bytes 4718596
  285.8 99.2 %copy-start.5 = (bf16[6,4096]{1,0:T(8,128)(2,1)S(1)}, bf16[6,4096]{1,0:T(8,128)(2,1)}, u32[]{:S(2)}) copy-start(bf16[6,4096]{1,0:T(8,128)(2,1)} %param.16) | copy-start | bytes 147460
  285.8 99.2 %copy-start.6 = (f32[4096]{0:T(1024)S(1)}, f32[4096]{0:T(1024)}, u32[]{:S(2)}) copy-start(f32[4096]{0:T(1024)} %param.28) | copy-start | bytes 49156
  285.8 99.1 %copy-start.7 = (f32[4096]{0:T(1024)S(1)}, f32[4096]{0:T(1024)}, u32[]{:S(2)}) copy-start(f32[4096]{0:T(1024)} %param.24) | copy-start | bytes 49156
Sparse Core Ops, SparseCore 0:
  10.5 63.1 all-gather.6
  75.7 169.9 all-gather.4
  287.6 97.3 reduce-scatter.1
where the time goes:
time: 393 us
  waiting for transfers between devices  323 us (82%)
  local copies, waits for them, and re-layouts  28.1 us (7%)
  matrix products  18.4 us (5%)
  between operations  13.4 us (3%)
  other arithmetic  9.59 us (2%)
    all_gather x1, waiting for transfers between devices, body(): gathered = lax.all_gather(packed, 'tok', axis=0, tiled=False)  164 us
    reduce_scatter x1, waiting for transfers between devices, body(): lax.psum_scatter(partial, 'head', scatter_dimension=0, tiled=True)  97.5 us
    all_gather x1, waiting for transfers between devices, body(): whole = lax.all_gather(tokens, 'head', axis=0, tiled=True)  61.5 us
    unnamed x37, local copies, waits for them, and re-layouts  21.5 us
    dot_general x1, matrix products, body(): lax.dot_general(hidden, down_t, contract, preferred_element_type=jnp.floa...  8.67 us
  transfers between devices with their start and end apart: 3, of which 3 were waited for; matrix products, arithmetic and copies ran while one was open for 3% of the time, Pallas kernels for 0%

commit v1 on v0

--- a/solution.py
+++ b/solution.py
@@ -90,7 +90,9 @@
     offset = width_qkv + width_up
     dense_t = gathered[:, :, offset : offset + width_dense].reshape(parts, width_dense)
     down_t = gathered[:, :, offset + width_dense :].reshape(parts, -1)
-    whole = lax.all_gather(tokens, "head", axis=0, tiled=True)
+    whole = jnp.concatenate(
+        lax.all_to_all(jnp.stack([tokens] * lax.axis_size("head")), "head", 0, 0), axis=0
+    )
     normed_one = layer_norm(whole, ln1_gain, ln1_bias).astype(jnp.bfloat16)
     normed_two = layer_norm(whole, ln2_gain, ln2_bias).astype(jnp.bfloat16)
     rows_total = whole.shape[0]

time: 393 us -> 336 us (0.85)
  waiting for transfers between devices: 323 us -> 243 us
  starting transfers between devices: 0.08 us -> 10.4 us
  local copies, waits for them, and re-layouts: 28.1 us -> 34.5 us
  other arithmetic: 9.59 us -> 14.9 us
    all_gather x1 -> x0, waiting for transfers between devices: 61.5 us -> none  [body(): whole = lax.all_gather(tokens, 'head', axis=0, tiled=True)]
    all_gather x1, waiting for transfers between devices: 164 us -> 118 us  [body(): gathered = lax.all_gather(packed, 'tok', axis=0, tiled=False)]
    all_to_all x0 -> x1, waiting for transfers between devices: none -> 27.2 us  [body(): lax.all_to_all(jnp.stack([tokens] * lax.axis_size('head')), 'head', 0, 0)]
    all_to_all x0 -> x1, starting transfers between devices: none -> 10.4 us  [body(): lax.all_to_all(jnp.stack([tokens] * lax.axis_size('head')), 'head', 0, 0)]
    convert_element_type x0 -> x1, other arithmetic: none -> 5.18 us  [body(): normed_two = layer_norm(whole, ln2_gain, ln2_bias).astype(jnp.bfloat16)]
    unnamed x37 -> x35, local copies, waits for them, and re-layouts: 21.5 us -> 21.3 us
  transfers between devices with their start and end apart: 3 -> 3, of which waited for: 3 -> 3; matrix products, arithmetic and copies ran while one was open for 3% -> 6% of each run, Pallas kernels for 0% -> 0%
where the time goes in v1:
time: 336 us; the launch traced here: 335 us
  waiting for transfers between devices  243 us (72%)
  local copies, waits for them, and re-layouts  34.5 us (10%)
  matrix products  18.9 us (6%)
  other arithmetic  14.9 us (4%)
  between operations  13.7 us (4%)
  starting transfers between devices  10.4 us (3%)
    all_gather x1, waiting for transfers between devices, body(): gathered = lax.all_gather(packed, 'tok', axis=0, tiled=False)  118 us
    reduce_scatter x1, waiting for transfers between devices, body(): lax.psum_scatter(partial, 'head', scatter_dimension=0, tiled=True)  97.5 us
    all_to_all x1, waiting for transfers between devices, body(): lax.all_to_all(jnp.stack([tokens] * lax.axis_size('head')), 'head', 0, 0)  27.2 us
    unnamed x35, local copies, waits for them, and re-layouts  21.3 us
    all_to_all x1, starting transfers between devices, body(): lax.all_to_all(jnp.stack([tokens] * lax.axis_size('head')), 'head', 0, 0)  10.4 us
    dot_general x1, matrix products, body(): lax.dot_general(hidden, down_t, contract, preferred_element_type=jnp.floa...  8.91 us
  transfers between devices with their start and end apart: 3, of which 3 were waited for; matrix products, arithmetic and copies ran while one was open for 6% of the time, Pallas kernels for 0%

profile of v1, /device:TPU:2, one launch (start us, length us, event | category | flops | bytes accessed | tf_op | source)
XLA Modules:
  0.0 335.1 jit_solution(15912548047222850350)
XLA Ops:
  6.5 1.2 copy.24
  7.7 1.1 copy.23
  8.8 1.9 pad_maximum_fusion
  10.8 2.4 stack.2
  13.2 10.4 %all-to-all-start = ((bf16[32,6,4096]{2,1,0:T(8,128)(2,1)}), bf16[32,6,4096]{2,1,0:T(8,128)(2,1)}, u32[]{:S(2)}, u32[]{:S(2)}) async-start(bf16[32,6,4096]{2,1,0:T(8,128)(2,1)} %stack.2), calls=%async_computation | async-start | bytes 4194304 | tf_op jit(solution)/shard_map/all_to_all | solution.py:94
  23.7 0.2 reduce-window_clone.1
  24.0 0.4 convert_reduce_fusion.1
  24.4 27.2 %all-to-all-done = bf16[32,6,4096]{2,1,0:T(8,128)(2,1)} async-done(((bf16[32,6,4096]{2,1,0:T(8,128)(2,1)}), bf16[32,6,4096]{2,1,0:T(8,128)(2,1)}, u32[]{:S(2)}, u32[]{:S(2)}) %all-to-all-start) | async-done | bytes 1572896 | tf_op jit(solution)/shard_map/all_to_all | solution.py:94
  51.6 2.1 convert_reduce_fusion
  53.7 2.4 fusion.12
  56.2 5.2 %fusion.11 = (bf16[32,6,4096]{2,1,0:T(8,128)(2,1)}, bf16[32,6,4096]{2,1,0:T(8,128)(2,1)}) fusion(bf16[32,6,4096]{2,1,0:T(8,128)(2,1)} %all-to-all-done, f32[4096]{0:T(1024)S(1)} %copy-done.5, f32[4096]{0:T(1024)S(1)} %copy-done.6, f32[32,6]{1,0:T(8,128)S(1)} %add_rsqrt_fusion, f32[32,6]{1,0:T(8,128)S(1)} %broadcast_multiply_fusion, f32[4096]{0:T(1024)S(1)} %copy-done.7, ...), kind=kLoop, calls=%fused_computation.17 | loop fusion | flops 7077888 | bytes 4785664 | tf_op jit(solution)/shard_map/convert_element_type | solution.py:97
  61.4 3.6 %convert_element_type.65 = bf16[192,4096]{1,0:T(8,128)(2,1)} reshape(bf16[32,6,4096]{2,1,0:T(8,128)(2,1)} %get-tuple-element.10) | data formatting | bytes 3145728 | tf_op jit(solution)/shard_map/convert_element_type | solution.py:96
  65.0 2.6 convert_element_type.71
  67.6 118.0 %all-gather.3.cloned.1.call-done = bf16[4096,1536]{0,1:T(8,128)(2,1)} async-done(((bf16[256,1536]{0,1:T(8,128)(2,1)}), bf16[4096,1536]{0,1:T(8,128)(2,1)}) %all-gather.3.cloned.1.call-update) | async-done | bytes 12582928 | tf_op jit(solution)/shard_map/all_gather | solution.py:86
  185.6 7.9 %copy.27 = bf16[192,8,16,256]{3,2,1,0:T(8,128)(2,1)S(1)} copy(bf16[192,8,16,256]{3,1,2,0:T(8,128)(2,1)} %bitcast.41) | data formatting | bytes 25165824
  193.6 0.2 slice.55
  193.8 1.5 copy.28
  195.3 1.0 fusion.141
  196.5 0.3 fusion.143
  196.7 2.7 fusion.142
  199.4 0.2 fusion.79
  199.7 0.8 fusion.139
  200.5 0.4 copy.29
  201.0 0.6 copy-done.2
  201.6 0.8 fusion.13
  202.4 4.3 %copy.31 = bf16[64,8,16,256]{3,1,2,0:T(8,128)(2,1)} copy(bf16[64,8,16,256]{3,2,1,0:T(8,128)(2,1)S(1)} %bitcast.40) | data formatting | bytes 8388608
  206.7 4.2 %copy.30 = bf16[64,8,16,256]{3,1,2,0:T(8,128)(2,1)} copy(bf16[64,8,16,256]{3,2,1,0:T(8,128)(2,1)S(1)} %bitcast.39) | data formatting | bytes 8388608
  210.9 5.9 %fusion.29 = f32[192,4096]{1,0:T(8,128)} fusion(bf16[4096,128]{0,1:T(8,128)(2,1)S(1)} %bitcast.43, f32[192,128]{1,0:T(8,128)S(1)} %fusion.79, bf16[6144,128]{1,0:T(8,128)(2,1)} %param.30, f32[192,6144]{1,0:T(8,128)} %copy-done.2, f32[192]{0:T(256)S(1)} %max.37, f32[192]{0:T(256)S(1)} %add.135), kind=kOutput, calls=%fused_computation.30 | convolution fusion | flops 505749504 | bytes 10585600 | tf_op jit(solution)/shard_map/dot_general | solution.py:126
  216.8 8.9 %fusion.1 = bf16[192,4096]{1,0:T(8,128)(2,1)} fusion(f32[192,4096]{1,0:T(8,128)} %fusion.29, bf16[4096,512]{0,1:T(8,128)(2,1)} %bitcast.44, bf16[192,4096]{1,0:T(8,128)(2,1)S(1)} %convert_element_type.71, bf16[4096,512]{0,1:T(8,128)(2,1)} %bitcast.45, f32[512]{0:T(512)S(1)} %copy-done.13), kind=kOutput, calls=%fused_computation.5 | convolution fusion | flops 1618673664 | bytes 14682112 | tf_op jit(solution)/shard_map/dot_general | solution.py:128
  225.7 3.5 %reshape.178 = bf16[32,6,4096]{2,1,0:T(8,128)(2,1)} reshape(bf16[192,4096]{1,0:T(8,128)(2,1)} %fusion.1) | data formatting | bytes 3145728 | tf_op jit(solution)/shard_map/reshape | solution.py:130
  229.3 97.5 %reduce-scatter.2.cloned.1.call-done = bf16[1,6,4096]{2,1,0:T(8,128)(2,1)} async-done(((bf16[32,6,4096]{2,1,0:T(8,128)(2,1)}), bf16[1,6,4096]{2,1,0:T(8,128)(2,1)}) %reduce-scatter.2.cloned.1.call-update) | async-done | bytes 49168 | tf_op jit(solution)/shard_map/reduce_scatter | solution.py:131
  326.7 1.5 fusion.78
  (47 shorter events, 0.6 us)
Async XLA Ops:
  6.5 190.2 %copy-start = (bf16[6144,128]{1,0:T(8,128)(2,1)S(1)}, bf16[6144,128]{1,0:T(8,128)(2,1)}, u32[]{:S(2)}) copy-start(bf16[6144,128]{1,0:T(8,128)(2,1)} %param.29) | copy-start | bytes 4718596
  6.5 179.0 %all-gather.3.cloned.1.call-start = ((), (), s32[]{:S(2)}) async-start(), calls=%async_computation.3 | async-start | bytes 13369344 | tf_op jit(solution)/shard_map/all_gather | solution.py:86
  8.8 14.9 %copy-start.11 = (s32[1,33]{1,0:T(1,128)S(1)}, s32[1,33]{1,0:T(1,128)}, u32[]{:S(2)}) copy-start(s32[1,33]{1,0:T(1,128)} %param.31) | copy-start | bytes 400
  13.2 43.0 %copy-start.5 = (f32[4096]{0:T(1024)S(1)}, f32[4096]{0:T(1024)}, u32[]{:S(2)}) copy-start(f32[4096]{0:T(1024)} %param.20) | copy-start | bytes 49156
  13.2 43.0 %copy-start.6 = (f32[4096]{0:T(1024)S(1)}, f32[4096]{0:T(1024)}, u32[]{:S(2)}) copy-start(f32[4096]{0:T(1024)} %param.19) | copy-start | bytes 49156
  13.2 43.0 %copy-start.7 = (f32[4096]{0:T(1024)S(1)}, f32[4096]{0:T(1024)}, u32[]{:S(2)}) copy-start(f32[4096]{0:T(1024)} %param.18) | copy-start | bytes 49156
  13.2 43.0 %copy-start.8 = (f32[4096]{0:T(1024)S(1)}, f32[4096]{0:T(1024)}, u32[]{:S(2)}) copy-start(f32[4096]{0:T(1024)} %param.17) | copy-start | bytes 49156
  13.2 38.4 %all-to-all-start = ((bf16[32,6,4096]{2,1,0:T(8,128)(2,1)}), bf16[32,6,4096]{2,1,0:T(8,128)(2,1)}, u32[]{:S(2)}, u32[]{:S(2)}) async-start(bf16[32,6,4096]{2,1,0:T(8,128)(2,1)} %stack.2), calls=%async_computation | async-start | bytes 4194304 | tf_op jit(solution)/shard_map/all_to_all | solution.py:94
  23.6 303.1 %reduce-scatter.2.cloned.1.call-start = ((), (), s32[]{:S(2)}) async-start(), calls=%async_computation.2 | async-start | bytes 2162688 | tf_op jit(solution)/shard_map/reduce_scatter | solution.py:131
  193.8 1.5 copy-start.3
  193.8 1.5 copy-start.12
  199.4 2.2 copy-start.2
  210.9 5.9 %copy-start.13 = (f32[512]{0:T(512)S(1)}, f32[512]{0:T(512)}, u32[]{:S(2)}) copy-start(f32[512]{0:T(512)} %param.26) | copy-start | bytes 6148
  216.8 111.5 %copy-start.1 = (bf16[6144,128]{1,0:T(8,128)(2,1)S(1)}, bf16[6144,128]{1,0:T(8,128)(2,1)}, u32[]{:S(2)}) copy-start(bf16[6144,128]{1,0:T(8,128)(2,1)} %param.29) | copy-start | bytes 4718596
  225.7 101.1 %copy-start.4 = (bf16[6,4096]{1,0:T(8,128)(2,1)S(1)}, bf16[6,4096]{1,0:T(8,128)(2,1)}, u32[]{:S(2)}) copy-start(bf16[6,4096]{1,0:T(8,128)(2,1)} %param.16) | copy-start | bytes 147460
  225.7 101.1 %copy-start.9 = (f32[4096]{0:T(1024)S(1)}, f32[4096]{0:T(1024)}, u32[]{:S(2)}) copy-start(f32[4096]{0:T(1024)} %param.28) | copy-start | bytes 49156
  225.7 101.1 %copy-start.10 = (f32[4096]{0:T(1024)S(1)}, f32[4096]{0:T(1024)}, u32[]{:S(2)}) copy-start(f32[4096]{0:T(1024)} %param.24) | copy-start | bytes 49156
Sparse Core Ops, SparseCore 0:
  10.9 174.6 all-gather.2
  229.4 97.3 reduce-scatter.1
